TPU v7x, 32 devices: a whole 2x2x4 slice. The times are simulated.
32 devices in a mesh: tok: 4 (over y, x), feat: 8 (over z, core).
Axes of the slice: x: 2, y: 2, z: 4, core: 2. Of those that a mesh axis runs over, the one named last changes fastest.
Arguments:
- acts: bfloat16 [512, 8192], P('tok', 'feat'), may hold values from -6 to 6
- grad_out: bfloat16 [512, 28672], P('tok', 'feat'), may hold values from -6 to 6
- weight: bfloat16 [8192, 28672], P('tok', 'feat'), may hold values from -0.03125 to 0.03125
- block_rows: int32 [1024], P('feat'), may hold values from 0 to 63
- block_cols: int32 [1024], P('feat'), may hold values from 0 to 27
- block_count: int32 [8], P('feat'), may hold values from 1 to 128, as said below
Outputs:
- grad_in: bfloat16 [512, 8192], P('feat', 'tok')
- block_grads: bfloat16 [1024, 128, 128], P('feat', 'tok')
Inputs may be any that keep to these rules, and one draw needn't show every extreme that they name: `block_count`: each feat shard lists at most 128 blocks; one shard lists exactly 128; listed blocks of a shard may repeat.
All inputs are finite; a program needn't handle non-finite values.
Results may differ from a plain program's by a relative error of at most 0.001.
Values may be sent and summed in bfloat16 or wider, within the bound.
No kernel may reach another device: no remote copies, remote signals or barrier semaphores. Data moves between devices by JAX's collectives and lax.ppermute only.
A program may use at most 128 MiB of HBM per device.

v0:
```python
import jax
import jax.numpy as jnp
from jax import lax
from jax.sharding import PartitionSpec as P

BLK = 128


def per_device(acts, grad_out, weight, block_rows, block_cols, block_count):
    tok_dev = acts.shape[0]
    slot_count = block_rows.shape[0]
    active = (jnp.arange(slot_count, dtype=jnp.int32) < block_count[0]).astype(jnp.float32)
    full_acts = lax.all_gather(acts, "feat", axis=1, tiled=True)
    row_blocks = full_acts.shape[1] // BLK
    partial_sums = lax.dot_general(
        lax.all_gather(grad_out, "tok", axis=0, tiled=True),
        weight,
        (((1,), (1,)), ((), ())),
        preferred_element_type=jnp.float32,
    )
    act_sel = jnp.take(full_acts.reshape(tok_dev, row_blocks, BLK), block_rows, axis=1)
    grad_sel = jnp.take(grad_out.reshape(tok_dev, -1, BLK), block_cols, axis=1)
    partial_tiles = jnp.einsum(
        "tsa,tsb->sab", act_sel, grad_sel, preferred_element_type=jnp.float32
    )
    partial_tiles = partial_tiles * active[:, None, None]
    block_grads = lax.psum_scatter(partial_tiles, "tok", scatter_dimension=1, tiled=True).astype(
        jnp.bfloat16
    )
    grad_in = lax.psum_scatter(partial_sums, "feat", scatter_dimension=0, tiled=True).astype(
        jnp.bfloat16
    )
    return (grad_in, block_grads)


def solution(mesh):
    in_specs = (
        P("tok", "feat"),
        P("tok", "feat"),
        P("tok", "feat"),
        P("feat"),
        P("feat"),
        P("feat"),
    )
    out_specs = (P("feat", "tok"), P("feat", "tok", None))
    return jax.shard_map(
        per_device, mesh=mesh, in_specs=in_specs, out_specs=out_specs, check_vma=False
    )
```

profile of v0, /device:TPU:0, one launch (start us, length us, event | category | flops | bytes accessed | tf_op | source)
XLA Modules:
  0.0 240.9 jit_solution(17467459685259097102)
XLA Ops:
  7.2 0.0 all-gather.3.cloned.1.call-start
  7.2 0.7 all-gather.3.cloned.1.call-update
  7.9 0.0 all-gather.5.cloned.1.call-start
  7.9 1.8 copy.12
  9.7 0.0 all-gather.5.cloned.1.call-update
  9.8 0.0 reduce-scatter.3.cloned.1.call-start
  9.8 51.1 %all-gather.3.cloned.1.call-done = bf16[512,3584]{1,0:T(8,128)(2,1)} async-done(((bf16[128,3584]{1,0:T(8,128)(2,1)}), bf16[512,3584]{1,0:T(8,128)(2,1)}) %all-gather.3.cloned.1.call-update) | async-done | bytes 3670032 | tf_op jit(solution)/shard_map/all_gather | solution.py:16
  60.9 13.5 %fusion.13 = f32[512,2048]{1,0:T(8,128)} fusion(bf16[512,3584]{1,0:T(8,128)(2,1)} %all-gather.3.cloned.1.call-done, bf16[2048,3584]{1,0:T(8,128)(2,1)} %param.8), kind=kOutput, calls=%fused_computation.19 | convolution fusion | flops 7516192768 | bytes 22544384 | tf_op jit(solution)/shard_map/dot_general | solution.py:15
  74.4 0.0 reduce-scatter.3.cloned.1.call-update
  74.5 0.0 reduce-scatter.5.cloned.1.call-start
  74.5 1.1 copy-done
  75.6 0.6 copy.14
  76.9 0.6 copy.15
  77.6 0.0 copy-start.2
  77.6 3.0 %gather_fusion.1 = bf16[128,128,128]{2,1,0:T(8,128)(2,1)} fusion(bf16[128,28,128]{2,0,1:T(8,128)(2,1)S(1)} %copy.15, s32[1024]{0:T(1024)S(1)} %pad_clamp_fusion), kind=kCustom, calls=%fused_computation.1 | custom fusion | bytes 8389120 | tf_op jit(solution)/shard_map/jit(_take)/gather | solution.py:22
  80.7 11.6 %all-gather.5.cloned.1.call-done = bf16[128,8192]{0,1:T(8,128)(2,1)} async-done(((bf16[128,1024]{0,1:T(8,128)(2,1)}), bf16[128,8192]{0,1:T(8,128)(2,1)}) %all-gather.5.cloned.1.call-update) | async-done | bytes 2097168 | tf_op jit(solution)/shard_map/all_gather | solution.py:13
  92.2 3.2 %copy.13 = bf16[128,64,128]{2,0,1:T(8,128)(2,1)S(1)} copy(bf16[128,64,128]{0,2,1:T(8,128)(2,1)} %bitcast.17) | data formatting | bytes 4194304 | tf_op jit(solution)/shard_map/reshape | solution.py:21
  95.4 3.0 %gather_fusion = bf16[128,128,128]{2,1,0:T(8,128)(2,1)} fusion(bf16[128,64,128]{2,0,1:T(8,128)(2,1)S(1)} %copy.13, s32[1024]{0:T(1024)S(1)} %pad_clamp_fusion.1), kind=kCustom, calls=%fused_computation | custom fusion | bytes 8389120 | tf_op jit(solution)/shard_map/jit(_take)/gather | solution.py:21
  98.5 9.4 %broadcast_multiply_fusion = f32[128,128,128]{2,1,0:T(8,128)} fusion(f32[128]{0:T(128)S(1)} %get-tuple-element.2, bf16[128,128,128]{2,1,0:T(8,128)(2,1)} %gather_fusion.1, pred[128]{0:T(512)(128)(4,1)S(1)} %get-tuple-element.3, bf16[128,128,128]{2,1,0:T(8,128)(2,1)} %gather_fusion, pred[128]{0:T(512)(128)(4,1)S(1)} %compare_and_fusion.1), kind=kOutput, calls=%fused_computation.7 | convolution fusion | flops 543162368 | bytes 16777984 | tf_op jit(solution)/shard_map/tsa,tsb->sab/dot_general | solution.py:23
  107.9 0.0 reduce-scatter.5.cloned.1.call-update
  107.9 36.2 %reduce-scatter.3.cloned.1.call-done = f32[64,2048]{1,0:T(8,128)} async-done(((f32[512,2048]{1,0:T(8,128)}), f32[64,2048]{1,0:T(8,128)}) %reduce-scatter.3.cloned.1.call-update) | async-done | bytes 524304 | tf_op jit(solution)/shard_map/reduce_scatter | solution.py:30
  144.1 1.8 convert_element_type.13
  145.8 85.7 %reduce-scatter.5.cloned.1.call-done = f32[128,32,128]{2,1,0:T(8,128)} async-done(((f32[128,128,128]{2,1,0:T(8,128)}), f32[128,32,128]{2,1,0:T(8,128)}) %reduce-scatter.5.cloned.1.call-update) | async-done | bytes 2097168 | tf_op jit(solution)/shard_map/reduce_scatter | solution.py:27
  231.6 2.8 %convert_element_type.15 = bf16[128,32,128]{2,1,0:T(8,128)(2,1)} convert(f32[128,32,128]{2,1,0:T(8,128)} %reduce-scatter.5.cloned.1.call-done) | non-fusion elementwise | flops 524288 | bytes 3145728 | tf_op jit(solution)/shard_map/convert_element_type | solution.py:27
  (10 shorter events, 0.0 us)
Async XLA Ops:
  7.2 53.8 %all-gather.3.cloned.1.call-start = ((), (), s32[]{:S(2)}) async-start(), calls=%async_computation.2 | async-start | bytes 4587520 | tf_op jit(solution)/shard_map/all_gather | solution.py:16
  7.9 84.3 %all-gather.5.cloned.1.call-start = ((), (), s32[]{:S(2)}) async-start(), calls=%async_computation.4 | async-start | bytes 2359296 | tf_op jit(solution)/shard_map/all_gather | solution.py:13
  9.8 134.3 %reduce-scatter.3.cloned.1.call-start = ((), (), s32[]{:S(2)}) async-start(), calls=%async_computation.3 | async-start | bytes 4718592 | tf_op jit(solution)/shard_map/reduce_scatter | solution.py:30
  74.4 1.2 copy-start
  74.4 3.1 %copy-start.1 = (s32[128]{0:T(128)S(1)}, s32[128]{0:T(128)}, u32[]{:S(2)}) copy-start(s32[128]{0:T(128)} %param.10) | copy-start | bytes 1540
  74.5 157.1 %reduce-scatter.5.cloned.1.call-start = ((), (), s32[]{:S(2)}) async-start(), calls=%async_computation.5 | async-start | bytes 10485760 | tf_op jit(solution)/shard_map/reduce_scatter | solution.py:27
  77.6 3.0 %copy-start.2 = (s32[128]{0:T(128)S(1)}, s32[128]{0:T(128)}, u32[]{:S(2)}) copy-start(s32[128]{0:T(128)} %param.9) | copy-start | bytes 1540
Sparse Core Ops, SparseCore 0:
  9.8 51.0 all-gather.2
  63.1 29.0 all-gather.4
  94.5 49.4 reduce-scatter.2
  147.0 84.5 reduce-scatter.4
where the time goes:
time: 241 us
  waiting for transfers between devices  185 us (77%)
  matrix products  22.9 us (10%)
  between operations  14.5 us (6%)
  local copies, waits for them, and re-layouts  13.4 us (6%)
  other arithmetic  4.59 us (2%)
    reduce_scatter x1, waiting for transfers between devices, per_device(): lax.psum_scatter(partial_tiles, 'tok', scatter_dimension=1, tiled=True)  85.7 us
    all_gather x1, waiting for transfers between devices, per_device(): lax.all_gather(grad_out, 'tok', axis=0, tiled=True)  51.1 us
    reduce_scatter x1, waiting for transfers between devices, per_device(): lax.psum_scatter(partial_sums, 'feat', scatter_dimension=0, tiled=True)  36.2 us
    dot_general x1, matrix products, per_device(): lax.dot_general(lax.all_gather(grad_out, 'tok', axis=0, tiled=True), weig...  13.5 us
    all_gather x1, waiting for transfers between devices, per_device(): full_acts = lax.all_gather(acts, 'feat', axis=1, tiled=True)  11.6 us
    dot_general x1, matrix products, per_device(): jnp.einsum('tsa,tsb->sab', act_sel, grad_sel, preferred_element_type=jnp....  9.38 us
  transfers between devices with their start and end apart: 4, of which 4 were waited for; matrix products, arithmetic and copies ran while one was open for 15% of the time, Pallas kernels for 0%

commit v1 on v0

--- a/solution.py
+++ b/solution.py
@@ -1,3 +1,4 @@
+import functools
 import jax
 import jax.numpy as jnp
 from jax import lax
@@ -6,11 +7,27 @@
 BLK = 128
 
 
+def _lay_sections(target, across, dim_k):
+    count_all = lax.psum(1, axis_name=across)
+    shelf = [(s, (s + 1) % count_all) for s in range(count_all)]
+    r_now = [None] * count_all
+    r_now[count_all - 1] = target
+    for at in range(count_all - 2, -1, -1):
+        r_now[at] = lax.ppermute(r_now[at + 1], axis_name=across, perm=shelf)
+    n_now = jnp.concatenate(r_now, dim_k)
+    arr_next = lax.axis_index(across)
+    value_now = (arr_next + 1) * target.shape[dim_k]
+    return jnp.roll(n_now, value_now, axis=dim_k)
+
+
+_fix_links = functools.partial(_lay_sections, across="feat", dim_k=1)
+
+
 def per_device(acts, grad_out, weight, block_rows, block_cols, block_count):
     tok_dev = acts.shape[0]
     slot_count = block_rows.shape[0]
     active = (jnp.arange(slot_count, dtype=jnp.int32) < block_count[0]).astype(jnp.float32)
-    full_acts = lax.all_gather(acts, "feat", axis=1, tiled=True)
+    full_acts = _fix_links(acts)
     row_blocks = full_acts.shape[1] // BLK
     partial_sums = lax.dot_general(
         lax.all_gather(grad_out, "tok", axis=0, tiled=True),

time: 241 us -> 266 us (1.10)
  waiting for transfers between devices: 185 us -> 207 us
  local copies, waits for them, and re-layouts: 13.4 us -> 17.4 us
    ppermute x0 -> x7, waiting for transfers between devices: none -> 69.9 us  [_lay_sections(): r_now[at] = lax.ppermute(r_now[at + 1], axis_name=across, perm=shelf)]
    reduce_scatter x1, waiting for transfers between devices: 36.2 us -> 0.02 us  [per_device(): lax.psum_scatter(partial_sums, 'feat', scatter_dimension=0, tiled=True)]
    all_gather x1 -> x0, waiting for transfers between devices: 11.6 us -> none  [per_device(): full_acts = lax.all_gather(acts, 'feat', axis=1, tiled=True)]
    reduce_scatter x1, waiting for transfers between devices: 85.7 us -> 83 us  [per_device(): lax.psum_scatter(partial_tiles, 'tok', scatter_dimension=1, tiled=True)]
    unnamed x8 -> x25, local copies, waits for them, and re-layouts: 3.52 us -> 5.98 us
  transfers between devices with their start and end apart: 4 -> 10, of which waited for: 4 -> 9; matrix products, arithmetic and copies ran while one was open for 15% -> 10% of each run, Pallas kernels for 0% -> 0%
where the time goes in v1:
time: 266 us
  waiting for transfers between devices  207 us (78%)
  matrix products  22.5 us (8%)
  local copies, waits for them, and re-layouts  17.4 us (7%)
  between operations  14.6 us (5%)
  other arithmetic  4.58 us (2%)
    reduce_scatter x1, waiting for transfers between devices, per_device(): lax.psum_scatter(partial_tiles, 'tok', scatter_dimension=1, tiled=True)  83 us
    ppermute x7, waiting for transfers between devices, _lay_sections(): r_now[at] = lax.ppermute(r_now[at + 1], axis_name=across, perm=shelf)  69.9 us
    all_gather x1, waiting for transfers between devices, per_device(): lax.all_gather(grad_out, 'tok', axis=0, tiled=True)  53 us
    dot_general x1, matrix products, per_device(): lax.dot_general(lax.all_gather(grad_out, 'tok', axis=0, tiled=True), weig...  13.5 us
    dot_general x1, matrix products, per_device(): jnp.einsum('tsa,tsb->sab', act_sel, grad_sel, preferred_element_type=jnp....  8.99 us
    unnamed x25, local copies, waits for them, and re-layouts  5.98 us
  transfers between devices with their start and end apart: 10, of which 9 were waited for; matrix products, arithmetic and copies ran while one was open for 10% of the time, Pallas kernels for 0%

profile of v1, /device:TPU:0, one launch (start us, length us, event | category | flops | bytes accessed | tf_op | source)
XLA Modules:
  0.0 265.9 jit_solution(7186139740724737192)
XLA Ops:
  7.2 0.7 all-gather.2.cloned.1.call-update
  7.9 53.0 %all-gather.2.cloned.1.call-done = bf16[512,3584]{1,0:T(8,128)(2,1)} async-done(((bf16[128,3584]{1,0:T(8,128)(2,1)}), bf16[512,3584]{1,0:T(8,128)(2,1)}) %all-gather.2.cloned.1.call-update) | async-done | bytes 3670032 | tf_op jit(solution)/shard_map/all_gather | solution.py:33
  60.9 13.5 %fusion.13 = f32[512,2048]{1,0:T(8,128)} fusion(bf16[512,3584]{1,0:T(8,128)(2,1)} %all-gather.2.cloned.1.call-done, bf16[2048,3584]{1,0:T(8,128)(2,1)} %param.8), kind=kOutput, calls=%fused_computation.36 | convolution fusion | flops 7516192768 | bytes 22544384 | tf_op jit(solution)/shard_map/dot_general | solution.py:32
  74.5 0.9 copy-done.1
  75.6 7.6 %collective-permute-done = bf16[128,1024]{0,1:T(8,128)(2,1)S(1)} collective-permute-done((bf16[128,1024]{0,1:T(8,128)(2,1)S(1)}, bf16[128,1024]{0,1:T(8,128)(2,1)S(1)}, u32[]{:S(2)}, u32[]{:S(2)}) %collective-permute-start) | collective-permute-done | bytes 262176 | tf_op jit(solution)/shard_map/ppermute | solution.py:16
  83.2 13.2 %collective-permute-done.1 = bf16[128,1024]{0,1:T(8,128)(2,1)S(1)} collective-permute-done((bf16[128,1024]{0,1:T(8,128)(2,1)S(1)}, bf16[128,1024]{0,1:T(8,128)(2,1)S(1)}, u32[]{:S(2)}, u32[]{:S(2)}) %collective-permute-start.1) | collective-permute-done | bytes 262176 | tf_op jit(solution)/shard_map/ppermute | solution.py:16
  96.4 13.4 %collective-permute-done.2 = bf16[128,1024]{0,1:T(8,128)(2,1)S(1)} collective-permute-done((bf16[128,1024]{0,1:T(8,128)(2,1)S(1)}, bf16[128,1024]{0,1:T(8,128)(2,1)S(1)}, u32[]{:S(2)}, u32[]{:S(2)}) %collective-permute-start.2) | collective-permute-done | bytes 262176 | tf_op jit(solution)/shard_map/ppermute | solution.py:16
  109.8 13.4 %collective-permute-done.3 = bf16[128,1024]{0,1:T(8,128)(2,1)S(1)} collective-permute-done((bf16[128,1024]{0,1:T(8,128)(2,1)S(1)}, bf16[128,1024]{0,1:T(8,128)(2,1)S(1)}, u32[]{:S(2)}, u32[]{:S(2)}) %collective-permute-start.3) | collective-permute-done | bytes 262176 | tf_op jit(solution)/shard_map/ppermute | solution.py:16
  123.2 11.8 %collective-permute-done.4 = bf16[128,1024]{0,1:T(8,128)(2,1)S(1)} collective-permute-done((bf16[128,1024]{0,1:T(8,128)(2,1)S(1)}, bf16[128,1024]{0,1:T(8,128)(2,1)S(1)}, u32[]{:S(2)}, u32[]{:S(2)}) %collective-permute-start.4) | collective-permute-done | bytes 262176 | tf_op jit(solution)/shard_map/ppermute | solution.py:16
  135.1 7.7 %collective-permute-done.5 = bf16[128,1024]{0,1:T(8,128)(2,1)} collective-permute-done((bf16[128,1024]{0,1:T(8,128)(2,1)S(1)}, bf16[128,1024]{0,1:T(8,128)(2,1)}, u32[]{:S(2)}, u32[]{:S(2)}) %collective-permute-start.5) | collective-permute-done | bytes 262176 | tf_op jit(solution)/shard_map/ppermute | solution.py:16
  143.4 0.6 copy.17
  144.7 3.0 %gather_fusion.1 = bf16[128,128,128]{2,1,0:T(8,128)(2,1)} fusion(bf16[128,28,128]{2,0,1:T(8,128)(2,1)S(1)} %copy.17, s32[1024]{0:T(1024)S(1)} %get-tuple-element.2), kind=kCustom, calls=%fused_computation.1 | custom fusion | bytes 8389120 | tf_op jit(solution)/shard_map/jit(_take)/gather | solution.py:39
  147.7 2.9 %collective-permute-done.6 = bf16[128,1024]{0,1:T(8,128)(2,1)} collective-permute-done((bf16[128,1024]{0,1:T(8,128)(2,1)}, bf16[128,1024]{0,1:T(8,128)(2,1)}, u32[]{:S(2)}, u32[]{:S(2)}) %collective-permute-start.6) | collective-permute-done | bytes 262176 | tf_op jit(solution)/shard_map/ppermute | solution.py:16
  150.6 1.0 constant_dynamic-update-slice_fusion.15
  151.6 1.0 constant_dynamic-update-slice_fusion.14
  152.9 1.0 constant_dynamic-update-slice_fusion.7
  153.8 1.0 constant_dynamic-update-slice_fusion.6
  155.1 1.5 constant_dynamic-slice_fusion
  156.6 3.2 %copy.15 = bf16[128,64,128]{2,0,1:T(8,128)(2,1)S(1)} copy(bf16[128,64,128]{0,2,1:T(8,128)(2,1)} %bitcast.16) | data formatting | bytes 4194304 | tf_op jit(solution)/shard_map/reshape | solution.py:38
  159.8 3.0 %gather_fusion = bf16[128,128,128]{2,1,0:T(8,128)(2,1)} fusion(bf16[128,64,128]{2,0,1:T(8,128)(2,1)S(1)} %copy.15, s32[1024]{0:T(1024)S(1)} %get-tuple-element.3), kind=kCustom, calls=%fused_computation | custom fusion | bytes 8389120 | tf_op jit(solution)/shard_map/jit(_take)/gather | solution.py:38
  162.8 9.0 %broadcast_multiply_fusion = f32[128,128,128]{2,1,0:T(8,128)} fusion(f32[128]{0:T(128)S(1)} %get-tuple-element.4, bf16[128,128,128]{2,1,0:T(8,128)(2,1)} %gather_fusion.1, pred[128]{0:T(512)(128)(4,1)S(1)} %get-tuple-element.5, bf16[128,128,128]{2,1,0:T(8,128)(2,1)} %gather_fusion, pred[128]{0:T(512)(128)(4,1)S(1)} %compare_and_fusion.1), kind=kOutput, calls=%fused_computation.7 | convolution fusion | flops 543162368 | bytes 16777984 | tf_op jit(solution)/shard_map/tsa,tsb->sab/dot_general | solution.py:40
  171.9 1.8 convert_element_type.13
  173.7 83.0 %reduce-scatter.5.cloned.1.call-done = f32[128,32,128]{2,1,0:T(8,128)} async-done(((f32[128,128,128]{2,1,0:T(8,128)}), f32[128,32,128]{2,1,0:T(8,128)}) %reduce-scatter.5.cloned.1.call-update) | async-done | bytes 2097168 | tf_op jit(solution)/shard_map/reduce_scatter | solution.py:44
  256.6 2.8 %convert_element_type.15 = bf16[128,32,128]{2,1,0:T(8,128)(2,1)} convert(f32[128,32,128]{2,1,0:T(8,128)} %reduce-scatter.5.cloned.1.call-done) | non-fusion elementwise | flops 524288 | bytes 3145728 | tf_op jit(solution)/shard_map/convert_element_type | solution.py:44
  (39 shorter events, 1.5 us)
Async XLA Ops:
  7.2 53.8 %all-gather.2.cloned.1.call-start = ((), (), s32[]{:S(2)}) async-start(), calls=%async_computation.2 | async-start | bytes 4587520 | tf_op jit(solution)/shard_map/all_gather | solution.py:33
  7.9 164.0 %reduce-scatter.3.cloned.1.call-start = ((), (), s32[]{:S(2)}) async-start(), calls=%async_computation.3 | async-start | bytes 4718592 | tf_op jit(solution)/shard_map/reduce_scatter | solution.py:47
  74.5 0.9 copy-start.1
  74.5 48.7 %copy-start.3 = (s32[128]{0:T(128)S(1)}, s32[128]{0:T(128)}, u32[]{:S(2)}) copy-start(s32[128]{0:T(128)} %param.9) | copy-start | bytes 1540
  74.5 60.6 %copy-start.2 = (s32[128]{0:T(128)S(1)}, s32[128]{0:T(128)}, u32[]{:S(2)}) copy-start(s32[128]{0:T(128)} %param.10) | copy-start | bytes 1540
  74.5 68.3 %copy-start = (bf16[128,3584]{1,0:T(8,128)(2,1)S(1)}, bf16[128,3584]{1,0:T(8,128)(2,1)}, u32[]{:S(2)}) copy-start(bf16[128,3584]{1,0:T(8,128)(2,1)} %param.7) | copy-start | bytes 2752516
  74.5 182.1 %reduce-scatter.5.cloned.1.call-start = ((), (), s32[]{:S(2)}) async-start(), calls=%async_computation.4 | async-start | bytes 10485760 | tf_op jit(solution)/shard_map/reduce_scatter | solution.py:44
  75.6 7.7 %collective-permute-start = (bf16[128,1024]{0,1:T(8,128)(2,1)S(1)}, bf16[128,1024]{0,1:T(8,128)(2,1)S(1)}, u32[]{:S(2)}, u32[]{:S(2)}) collective-permute-start(bf16[128,1024]{0,1:T(8,128)(2,1)S(1)} %copy.12), channel_id=1, source_target_pairs={{0,1},{1,2},{2,3},{3,4},{4,5},{5,6},{6,7},{7,0},{8,9},{9,10},{10,1... | collective-permute-start | bytes 786440 | tf_op jit(solution)/shard_map/ppermute | solution.py:16
  83.2 13.2 %collective-permute-start.1 = (bf16[128,1024]{0,1:T(8,128)(2,1)S(1)}, bf16[128,1024]{0,1:T(8,128)(2,1)S(1)}, u32[]{:S(2)}, u32[]{:S(2)}) collective-permute-start(bf16[128,1024]{0,1:T(8,128)(2,1)S(1)} %collective-permute-done), channel_id=1, source_target_pairs={{0,1},{1,2},{2,3},{3,4},{4,5},{5,6},{6,7},{7,0},{8,9},{9,10},{10,1... | collective-permute-start | bytes 786440 | tf_op jit(solution)/shard_map/ppermute | solution.py:16
  96.4 13.4 %collective-permute-start.2 = (bf16[128,1024]{0,1:T(8,128)(2,1)S(1)}, bf16[128,1024]{0,1:T(8,128)(2,1)S(1)}, u32[]{:S(2)}, u32[]{:S(2)}) collective-permute-start(bf16[128,1024]{0,1:T(8,128)(2,1)S(1)} %collective-permute-done.1), channel_id=1, source_target_pairs={{0,1},{1,2},{2,3},{3,4},{4,5},{5,6},{6,7},{7,0},{8,9},{9,10},{10,1... | collective-permute-start | bytes 786440 | tf_op jit(solution)/shard_map/ppermute | solution.py:16
  109.8 13.4 %collective-permute-start.3 = (bf16[128,1024]{0,1:T(8,128)(2,1)S(1)}, bf16[128,1024]{0,1:T(8,128)(2,1)S(1)}, u32[]{:S(2)}, u32[]{:S(2)}) collective-permute-start(bf16[128,1024]{0,1:T(8,128)(2,1)S(1)} %collective-permute-done.2), channel_id=1, source_target_pairs={{0,1},{1,2},{2,3},{3,4},{4,5},{5,6},{6,7},{7,0},{8,9},{9,10},{10,1... | collective-permute-start | bytes 786440 | tf_op jit(solution)/shard_map/ppermute | solution.py:16
  123.2 11.8 %collective-permute-start.4 = (bf16[128,1024]{0,1:T(8,128)(2,1)S(1)}, bf16[128,1024]{0,1:T(8,128)(2,1)S(1)}, u32[]{:S(2)}, u32[]{:S(2)}) collective-permute-start(bf16[128,1024]{0,1:T(8,128)(2,1)S(1)} %collective-permute-done.3), channel_id=1, source_target_pairs={{0,1},{1,2},{2,3},{3,4},{4,5},{5,6},{6,7},{7,0},{8,9},{9,10},{10,1... | collective-permute-start | bytes 786440 | tf_op jit(solution)/shard_map/ppermute | solution.py:16
  135.0 7.7 %collective-permute-start.5 = (bf16[128,1024]{0,1:T(8,128)(2,1)S(1)}, bf16[128,1024]{0,1:T(8,128)(2,1)}, u32[]{:S(2)}, u32[]{:S(2)}) collective-permute-start(bf16[128,1024]{0,1:T(8,128)(2,1)S(1)} %collective-permute-done.4), channel_id=1, source_target_pairs={{0,1},{1,2},{2,3},{3,4},{4,5},{5,6},{6,7},{7,0},{8,9},{9,10},{10,1... | collective-permute-start | bytes 786440 | tf_op jit(solution)/shard_map/ppermute | solution.py:16
  142.7 7.9 %collective-permute-start.6 = (bf16[128,1024]{0,1:T(8,128)(2,1)}, bf16[128,1024]{0,1:T(8,128)(2,1)}, u32[]{:S(2)}, u32[]{:S(2)}) collective-permute-start(bf16[128,1024]{0,1:T(8,128)(2,1)} %collective-permute-done.5), channel_id=1, source_target_pairs={{0,1},{1,2},{2,3},{3,4},{4,5},{5,6},{6,7},{7,0},{8,9},{9,10},{10,1... | collective-permute-start | bytes 786440 | tf_op jit(solution)/shard_map/ppermute | solution.py:16
Sparse Core Ops, SparseCore 0:
  9.8 51.0 all-gather.1
  74.6 60.3 reduce-scatter.2
  172.0 84.5 reduce-scatter.4
